TPU v7x, 32 devices: a whole 2x2x4 slice. The times are simulated.
32 devices in a mesh: seq: 16 (over z, y, x), tp: 2 (over core).
Axes of the slice: x: 2, y: 2, z: 4, core: 2. Of those that a mesh axis runs over, the one named last changes fastest.
Arguments:
- prefill_hidden: bfloat16 [2048, 5120], P('seq', 'tp'), may hold values from -14 to 14
- prefill_query_rows: bfloat16 [2048, 5120], P('seq', 'tp'), may hold values from -250 to 250
- prefill_key_value: bfloat16 [2, 2048, 1024], P(None, 'seq', 'tp'), may hold values from -5 to 5
- request_prefix_cache: bfloat16 [2, 16, 768, 1024], P(None, 'seq', None, 'tp'), may hold values from -5 to 5
- prefix_lengths: int32 [16], replicated, may hold values from 0 to 768, as said below
- decode_hidden: bfloat16 [4, 5120], P(None, 'tp'), may hold values from -14 to 14
- decode_query_rows: bfloat16 [4, 5120], P(None, 'tp'), may hold values from -250 to 250
- decode_kv: bfloat16 [2, 4, 1024], P(None, None, 'tp'), may hold values from -5 to 5
- decode_slot_cache: bfloat16 [2, 5, 2048, 1024], P(None, None, 'seq', 'tp'), may hold values from -5 to 5
- cache_lengths: int32 [4], replicated, may hold values from 512 to 2048, as said below
- slot_table: int32 [4], replicated, may hold values from 0 to 4, as said below
- out_weight: bfloat16 [5120, 5120], P('tp', 'seq'), may hold values from -0.078125 to 0.078125
- final_gain: bfloat16 [5120], replicated, may hold values from 0.5 to 1.5
- head_weight: bfloat16 [5120, 152064], P(None, ('seq', 'tp')), may hold values from -4 to 4
Outputs:
- prefill_out: bfloat16 [2048, 5120], P('seq', 'tp')
- decode_out: bfloat16 [4, 5120], P(None, 'tp')
- log_probs: float32 [20, 152064], P(None, ('seq', 'tp'))
Inputs may be any that keep to these rules, and one draw needn't show every extreme that they name: `prefix_lengths`: some request has no cached prefix and some has exactly 768 cached tokens. `cache_lengths`: some request has exactly 2048 cached tokens. `slot_table`: distinct slots.
All inputs are finite; a program needn't handle non-finite values.
Results may differ from a plain program's by a relative error of at most 0.0035.
Values may be sent and summed in bfloat16 or wider, within the bound.
No kernel may reach another device: no remote copies, remote signals or barrier semaphores. Data moves between devices by JAX's collectives and lax.ppermute only.
A program may use at most 128 MiB of HBM per device.

v0:
```python
import math
import jax
import jax.numpy as jnp
from jax import lax
from jax.sharding import PartitionSpec as P

QUERY_HEADS = 40
KEY_HEADS = 8
HEAD_SIZE = 128
neg_large = -1e30
exact = lax.Precision.HIGHEST
norm_eps = 1e-06


def merged(value, axis, join):
    pieces = jax.tree.map(lambda part: lax.all_gather(part, axis), value)
    head = jax.tree.map(lambda part: part[0], pieces)
    tail = jax.tree.map(lambda part: part[1:], pieces)
    subtotal, _ = lax.scan(lambda subtotal, piece: (join(subtotal, piece), None), head, tail)
    return subtotal


def join_parts(earlier, later):
    row_max = jnp.maximum(earlier[0], later[0])
    factor_one = jnp.exp(earlier[0] - row_max)
    factor_two = jnp.exp(later[0] - row_max)
    return (
        row_max,
        earlier[1] * factor_one + later[1] * factor_two,
        earlier[2] * factor_one[..., None] + later[2] * factor_two[..., None],
    )


def join_totals(earlier, later):
    row_max = jnp.maximum(earlier[0], later[0])
    return (
        row_max,
        earlier[1] * jnp.exp(earlier[0] - row_max) + later[1] * jnp.exp(later[0] - row_max),
    )


def local(
    prefill_hidden,
    prefill_query_rows,
    prefill_key_value,
    request_prefix_cache,
    prefix_lengths,
    decode_hidden,
    decode_query_rows,
    decode_kv,
    decode_slot_cache,
    cache_lengths,
    slot_table,
    out_weight,
    final_gain,
    head_weight,
):
    query_group_width = QUERY_HEADS // KEY_HEADS
    score_scale = 1.0 / math.sqrt(HEAD_SIZE)
    kv_local = prefill_key_value.shape[2] // HEAD_SIZE
    seq_index = lax.axis_index("seq")
    span_len = prefill_query_rows.shape[0]
    prefix_len = request_prefix_cache.shape[2]
    prefix_end = lax.dynamic_slice_in_dim(prefix_lengths, seq_index, 1)[0]
    query_matrix = prefill_query_rows.reshape(span_len, kv_local, query_group_width, HEAD_SIZE)
    joined_keys = jnp.concatenate([request_prefix_cache[0, 0], prefill_key_value[0]], 0).reshape(
        prefix_len + span_len, kv_local, HEAD_SIZE
    )
    value_matrix = jnp.concatenate([request_prefix_cache[1, 0], prefill_key_value[1]], 0).reshape(
        prefix_len + span_len, kv_local, HEAD_SIZE
    )
    key_place = jnp.arange(prefix_len + span_len)
    query_place = jnp.arange(span_len)
    live_mask = jnp.where(
        key_place[None, :] < prefix_len,
        key_place[None, :] < prefix_end,
        key_place[None, :] - prefix_len <= query_place[:, None],
    )
    scores = (
        jnp.einsum("rkgh,skh->kgrs", query_matrix, joined_keys, preferred_element_type=jnp.float32)
        * score_scale
    )
    masked = jnp.where(live_mask, scores, neg_large)
    row_max = jnp.max(masked, axis=-1, keepdims=True)
    weights = jnp.where(live_mask, jnp.exp(masked - row_max), 0.0)
    row_sum = jnp.sum(weights, axis=-1)
    weights_low = weights.astype(jnp.bfloat16)
    mixed = jnp.einsum(
        "kgrs,skh->rkgh", weights_low, value_matrix, preferred_element_type=jnp.float32
    )
    prefill_attention = (
        (mixed / jnp.transpose(row_sum, (2, 0, 1))[..., None])
        .astype(jnp.bfloat16)
        .reshape(span_len, -1)
    )
    decode_count = decode_query_rows.shape[0]
    ctx_local = decode_slot_cache.shape[2]
    chosen = jnp.take(decode_slot_cache, slot_table, axis=1)
    positions = seq_index * ctx_local + jnp.arange(ctx_local)
    decode_live = (positions[None, :] < cache_lengths[:, None])[:, None, None, :]
    decode_token_rows = decode_query_rows.reshape(
        decode_count, kv_local, query_group_width, HEAD_SIZE
    )
    cache_keys = chosen[0].reshape(decode_count, ctx_local, kv_local, HEAD_SIZE)
    cache_values = chosen[1].reshape(decode_count, ctx_local, kv_local, HEAD_SIZE)
    decode_scores = (
        jnp.einsum(
            "bkgh,bskh->bkgs", decode_token_rows, cache_keys, preferred_element_type=jnp.float32
        )
        * score_scale
    )
    decode_masked = jnp.where(decode_live, decode_scores, neg_large)
    decode_max = jnp.max(decode_masked, axis=-1)
    decode_weights = jnp.where(decode_live, jnp.exp(decode_masked - decode_max[..., None]), 0.0)
    decode_sum = jnp.sum(decode_weights, axis=-1)
    decode_mixed = jnp.einsum(
        "bkgs,bskh->bkgh", decode_weights, cache_values.astype(jnp.float32), precision=exact
    )
    best = lax.pmax(decode_max, "seq")
    factors = jnp.exp(decode_max - best)
    totals, mixtures = lax.psum((decode_sum * factors, decode_mixed * factors[..., None]), "seq")
    combined = (best, totals, mixtures)
    own_keys = decode_kv[0].reshape(decode_count, kv_local, HEAD_SIZE)
    own_values = decode_kv[1].reshape(decode_count, kv_local, HEAD_SIZE).astype(jnp.float32)
    own_scores = (
        jnp.einsum("bkgh,bkh->bkg", decode_token_rows, own_keys, preferred_element_type=jnp.float32)
        * score_scale
    )
    own_mixed = jnp.broadcast_to(own_values[:, :, None, :], combined[2].shape)
    final_max, final_sum, final_mixed = join_parts(
        combined, (own_scores, jnp.ones_like(own_scores), own_mixed)
    )
    decode_attention = (
        (final_mixed / final_sum[..., None]).astype(jnp.bfloat16).reshape(decode_count, -1)
    )
    attention_all = jnp.concatenate([prefill_attention, decode_attention], 0)
    every_row = lax.all_gather(attention_all, "seq", axis=0, tiled=True)
    column_block = jnp.dot(every_row, out_weight, preferred_element_type=jnp.float32)
    partial_terms = lax.all_to_all(column_block, "seq", split_axis=0, concat_axis=1, tiled=True)
    summed = lax.psum_scatter(partial_terms, "tp", scatter_dimension=1, tiled=True)
    residual = jnp.concatenate([prefill_hidden, decode_hidden], 0).astype(jnp.float32)
    updated = (residual + summed).astype(jnp.bfloat16)
    prefill_out = updated[:span_len]
    decode_out = updated[span_len:]
    gathered = lax.all_gather(prefill_out[span_len - 1 :], ("seq", "tp"), axis=0, tiled=True)
    decode_full = lax.all_gather(decode_out, "tp", axis=1, tiled=True)
    n_seq = lax.axis_size("seq")
    n_tp = lax.axis_size("tp")
    feature_width = prefill_out.shape[1]
    prefill_full = gathered.reshape(n_seq, n_tp * feature_width)
    head_input = jnp.concatenate([decode_full, prefill_full], 0).astype(jnp.float32)
    mean_square = jnp.mean(head_input * head_input, axis=-1, keepdims=True)
    normed = (
        head_input * lax.rsqrt(mean_square + norm_eps) * final_gain.astype(jnp.float32)
    ).astype(jnp.bfloat16)
    logits = jnp.dot(normed, head_weight, preferred_element_type=jnp.float32)
    local_max = jnp.max(logits, axis=-1)
    local_sum = jnp.sum(jnp.exp(logits - local_max[:, None]), axis=-1)
    global_max, global_sum = merged((local_max, local_sum), ("seq", "tp"), join_totals)
    log_probs = logits - (global_max + jnp.log(global_sum))[:, None]
    return (prefill_out, decode_out, log_probs)


def solution(mesh):
    return jax.shard_map(
        local,
        mesh=mesh,
        in_specs=(
            P("seq", "tp"),
            P("seq", "tp"),
            P(None, "seq", "tp"),
            P(None, "seq", None, "tp"),
            P(),
            P(None, "tp"),
            P(None, "tp"),
            P(None, None, "tp"),
            P(None, None, "seq", "tp"),
            P(),
            P(),
            P("tp", "seq"),
            P(),
            P(None, ("seq", "tp")),
        ),
        out_specs=(P("seq", "tp"), P(None, "tp"), P(None, ("seq", "tp"))),
        check_vma=False,
    )
```

profile of v0, /device:TPU:10, one launch (start us, length us, event | category | flops | bytes accessed | tf_op | source)
XLA Modules:
  0.0 531.2 jit_solution(17046051987952885032)
XLA Ops:
  8.7 1.9 gather_fusion
  11.7 31.6 %pmax.7 = f32[4,4,5]{2,1,0:T(4,128)S(1)} all-reduce(f32[4,4,5]{2,1,0:T(4,128)S(1)} %get-tuple-element.62), channel_id=1, replica_groups=mesh['seq'=16,'tp'=2] {'seq'}, use_global_device_ids=true, to_apply=%region_3.4 | all-reduce | flops 80 | bytes 640 | tf_op jit(solution)/shard_map/pmax | solution.py:119
  44.9 74.1 %all-reduce.3 = (f32[4,4,5,128]{3,2,1,0:T(8,128)S(1)}, f32[4,4,5]{2,1,0:T(4,128)S(1)}) all-reduce(f32[4,4,5,128]{3,2,1,0:T(8,128)S(1)} %convolution_multiply_fusion.1, f32[4,4,5]{2,1,0:T(4,128)S(1)} %bitcast.100), channel_id=1, replica_groups=mesh['seq'=16,'tp'=2] {'seq'}, use_global_device_ids=true, to_apply=%region_4.5 | all-reduce | flops 10320 | bytes 82560 | tf_op jit(solution)/shard_map/psum | solution.py:121
  120.4 2.4 fusion.55
  122.7 1.4 copy.77
  125.3 1.7 fusion.57
  128.8 2.2 copy.58
  132.9 1.4 fusion.31
  134.3 7.4 %fusion.59 = (f32[4,5,128]{2,1,0:T(8,128)S(1)}, bf16[4,5,128,896]{2,3,1,0:T(8,128)(2,1)}) fusion(pred[128,896]{0,1:T(8,128)(4,1)} %fusion.31, bf16[128,4,5,128]{0,3,2,1:T(8,128)(2,1)} %bitcast.92, bf16[128,4,128]{2,0,1:T(8,128)(2,1)S(1)} %copy-done.5, bf16[768,4,128]{2,0,1:T(8,128)(2,1)S(1)} %copy-done.2), kind=kOutput, calls=%fused_computation.82 | convolution fusion | flops 602801024 | bytes 6285312 | tf_op jit(solution)/shard_map/sub | solution.py:85
  141.8 4.1 fusion.18
  145.9 1.3 copy.65
  148.4 143.1 %all-gather.6.cloned.1.call-done = bf16[16,132,2560]{2,1,0:T(8,128)(2,1)} async-done(((bf16[1,132,2560]{2,1,0:T(8,128)(2,1)}), bf16[16,132,2560]{2,1,0:T(8,128)(2,1)}) %all-gather.6.cloned.1.call-update) | async-done | bytes 10813456 | tf_op jit(solution)/shard_map/all_gather | solution.py:137
  291.5 11.0 %reshape.134 = bf16[2112,2560]{1,0:T(8,128)(2,1)} reshape(bf16[16,132,2560]{2,1,0:T(8,128)(2,1)} %all-gather.6.cloned.1.call-done) | data formatting | bytes 21626880
  302.5 10.3 %fusion.62 = f32[2112,320]{1,0:T(8,128)} fusion(bf16[2112,2560]{1,0:T(8,128)(2,1)} %reshape.134, bf16[2560,320]{0,1:T(8,128)(2,1)S(1)} %copy-done), kind=kOutput, calls=%fused_computation.85 | convolution fusion | flops 3460300800 | bytes 15155200 | tf_op jit(solution)/shard_map/dot_general | solution.py:138
  312.8 4.2 all_to_all.14
  317.0 80.1 %all_to_all.19 = f32[16,132,320]{2,1,0:T(8,128)S(1)} all-to-all(f32[16,132,320]{2,1,0:T(8,128)} %all_to_all.14), channel_id=1, replica_groups=mesh['seq'=16,'tp'=2] {'seq'}, dimensions={0} | all-to-all | bytes 5406720 | tf_op jit(solution)/shard_map/all_to_all | solution.py:139
  397.1 2.3 copy.67
  399.4 4.8 all_to_all.17
  404.2 10.2 %reduce-scatter.2.cloned.1.call-done = f32[132,2560]{1,0:T(8,128)} async-done(((f32[132,5120]{1,0:T(8,128)}), f32[132,2560]{1,0:T(8,128)}) %reduce-scatter.2.cloned.1.call-update) | async-done | bytes 1351696 | tf_op jit(solution)/shard_map/reduce_scatter | solution.py:140
  414.4 1.5 add_convert_fusion
  415.9 31.5 %all-gather.3 = bf16[32,1,2560]{2,1,0:T(2,128)(2,1)S(1)} all-gather(bf16[1,1,2560]{2,1,0:T(2,128)(2,1)S(1)} %slice_bitcast_fusion), channel_id=1, replica_groups=mesh['seq'=16,'tp'=2] {'seq','tp'}, dimensions={0}, use_global_device_ids=true | all-gather | bytes 168960 | tf_op jit(solution)/shard_map/all_gather | solution.py:145
  448.4 1.8 all_gather.22
  450.5 19.8 %fusion.60 = (f32[20]{0:T(128)S(1)}, f32[20,4752]{1,0:T(8,128)S(1)}) fusion(bf16[5120,4752]{0,1:T(8,128)(2,1)} %param.29, f32[5120]{0:T(1024)S(1)} %convert_element_type.43, f32[20]{0:T(128)S(1)} %add_rsqrt_fusion, bf16[16,5120]{1,0:T(8,128)(2,1)S(1)} %reshape.110, bf16[4,5120]{1,0:T(4,128)(2,1)S(1)} %all_gather.22), kind=kOutput, calls=%fused_computation.83 | convolution fusion | flops 974021440 | bytes 49266080 | tf_op jit(solution)/shard_map/dot_general | solution.py:156
  471.0 49.9 %all-reduce.2 = (f32[640]{0:T(1024)S(1)}, f32[640]{0:T(1024)S(1)}) all-reduce(f32[640]{0:T(1024)S(1)} %dynamic-update-slice, f32[640]{0:T(1024)S(1)} %dynamic-update-slice.1), channel_id=2, replica_groups=mesh['seq'=16,'tp'=2] {'seq','tp'}, use_global_device_ids=true, to_apply=%add | all-reduce | flops 1280 | bytes 10240
  (115 shorter events, 17.8 us)
Async XLA Ops:
  7.2 295.3 %copy-start = (bf16[2560,320]{0,1:T(8,128)(2,1)S(1)}, bf16[2560,320]{0,1:T(8,128)(2,1)}, u32[]{:S(2)}) copy-start(bf16[2560,320]{0,1:T(8,128)(2,1)} %param.27) | copy-start | bytes 4915204
  7.2 284.3 %all-gather.6.cloned.1.call-start = ((), (), s32[]{:S(2)}) async-start(), calls=%async_computation.3 | async-start | bytes 11837440 | tf_op jit(solution)/shard_map/all_gather | solution.py:137
  8.7 2.5 copy-start.9
  8.7 2.6 copy-start.12
  10.7 33.1 %copy-start.11 = (bf16[2,4,512]{2,1,0:T(4,128)(2,1)S(1)}, bf16[2,4,512]{2,1,0:T(4,128)(2,1)}, u32[]{:S(2)}) copy-start(bf16[2,4,512]{2,1,0:T(4,128)(2,1)} %param.23) | copy-start | bytes 24580
  10.8 108.3 %copy-start.13 = (s32[16]{0:T(128)S(1)}, s32[16]{0:T(128)}, u32[]{:S(2)}) copy-start(s32[16]{0:T(128)} %param.20) | copy-start | bytes 196
  125.3 9.0 %copy-start.2 = (bf16[768,4,128]{2,0,1:T(8,128)(2,1)S(1)}, bf16[768,4,128]{2,0,1:T(8,128)(2,1)}, u32[]{:S(2)}) copy-start(bf16[768,4,128]{2,0,1:T(8,128)(2,1)} %copy.56) | copy-start | bytes 2359300
  128.8 5.5 %copy-start.5 = (bf16[128,4,128]{2,0,1:T(8,128)(2,1)S(1)}, bf16[128,4,128]{2,0,1:T(8,128)(2,1)}, u32[]{:S(2)}) copy-start(bf16[128,4,128]{2,0,1:T(8,128)(2,1)} %copy.57) | copy-start | bytes 393220
  134.3 7.5 %copy-start.3 = (bf16[1,1,768,512]{2,3,1,0:T(8,128)(2,1)S(1)}, bf16[1,1,768,512]{2,3,1,0:T(8,128)(2,1)}, u32[]{:S(2)}) copy-start(bf16[1,1,768,512]{2,3,1,0:T(8,128)(2,1)} %copy.52) | copy-start | bytes 2359300
  134.3 7.5 %copy-start.6 = (bf16[1,128,512]{1,2,0:T(8,128)(2,1)S(1)}, bf16[1,128,512]{1,2,0:T(8,128)(2,1)}, u32[]{:S(2)}) copy-start(bf16[1,128,512]{1,2,0:T(8,128)(2,1)} %copy.53) | copy-start | bytes 393220
  148.2 266.2 %reduce-scatter.2.cloned.1.call-start = ((), (), s32[]{:S(2)}) async-start(), calls=%async_computation.2 | async-start | bytes 4177920 | tf_op jit(solution)/shard_map/reduce_scatter | solution.py:140
  399.4 4.8 copy-start.10
  399.4 15.0 %copy-start.4 = (bf16[128,2560]{1,0:T(8,128)(2,1)S(1)}, bf16[128,2560]{1,0:T(8,128)(2,1)}, u32[]{:S(2)}) copy-start(bf16[128,2560]{1,0:T(8,128)(2,1)} %param.16) | copy-start | bytes 1966084
  399.4 15.0 %copy-start.8 = (bf16[4,2560]{1,0:T(4,128)(2,1)S(1)}, bf16[4,2560]{1,0:T(4,128)(2,1)}, u32[]{:S(2)}) copy-start(bf16[4,2560]{1,0:T(4,128)(2,1)} %param.21) | copy-start | bytes 61444
  415.9 54.4 %copy-start.7 = (bf16[4,2560]{1,0:T(4,128)(2,1)}, bf16[4,2560]{1,0:T(4,128)(2,1)S(1)}, u32[]{:S(2)}) copy-start(bf16[4,2560]{1,0:T(4,128)(2,1)S(1)} %slice.70) | copy-start | bytes 61444
  450.5 73.9 %copy-start.1 = (bf16[2560,320]{0,1:T(8,128)(2,1)S(1)}, bf16[2560,320]{0,1:T(8,128)(2,1)}, u32[]{:S(2)}) copy-start(bf16[2560,320]{0,1:T(8,128)(2,1)} %param.27) | copy-start | bytes 4915204
Sparse Core Ops, SparseCore 0:
  148.3 143.1 all-gather.5
  404.3 10.0 reduce-scatter.1
where the time goes:
time: 532 us; the launch traced here: 531 us
  blocking collectives  269 us (51%)
  waiting for transfers between devices  153 us (29%)
  matrix products  43.1 us (8%)
  local copies, waits for them, and re-layouts  41.2 us (8%)
  between operations  14.4 us (3%)
  other arithmetic  9.66 us (2%)
    all_gather x1, waiting for transfers between devices, local(): every_row = lax.all_gather(attention_all, 'seq', axis=0, tiled=True)  143 us
    all_to_all x1, blocking collectives, local(): lax.all_to_all(column_block, 'seq', split_axis=0, concat_axis=1, tiled=True)  80.1 us
    psum x1, blocking collectives, local(): lax.psum((decode_sum * factors, decode_mixed * factors[..., None]), 'seq')  74.1 us
    unnamed x1, blocking collectives  49.9 us
    pmax x1, blocking collectives, local(): best = lax.pmax(decode_max, 'seq')  31.6 us
    all_gather x1, blocking collectives, local(): lax.all_gather(prefill_out[span_len - 1:], ('seq', 'tp'), axis=0, tiled=T...  31.5 us
    dot_general x1, matrix products, local(): logits = jnp.dot(normed, head_weight, preferred_element_type=jnp.float32)  19.8 us
    unnamed x37, local copies, waits for them, and re-layouts  16.2 us
  transfers between devices with their start and end apart: 2, of which 2 were waited for; matrix products, arithmetic and copies ran while one was open for 0% of the time, Pallas kernels for 0%

commit v1 on v0

--- a/solution.py
+++ b/solution.py
@@ -134,7 +134,27 @@
         (final_mixed / final_sum[..., None]).astype(jnp.bfloat16).reshape(decode_count, -1)
     )
     attention_all = jnp.concatenate([prefill_attention, decode_attention], 0)
-    every_row = lax.all_gather(attention_all, "seq", axis=0, tiled=True)
+    peers, place, extent = (lax.axis_size("seq"), lax.axis_index("seq"), attention_all.shape[0])
+    ahead = [(i, (i + 1) % peers) for i in range(peers)]
+    behind = [(i, (i - 1) % peers) for i in range(peers)]
+    whole = jnp.zeros(
+        (*attention_all.shape[:0], peers * extent, *attention_all.shape[0 + 1 :]),
+        attention_all.dtype,
+    )
+    whole = lax.dynamic_update_slice_in_dim(whole, attention_all, place * extent, axis=0)
+    from_left = from_right = attention_all
+    half = peers // 2
+    for step in range(1, half + 1):
+        from_left = lax.ppermute(from_left, "seq", ahead)
+        whole = lax.dynamic_update_slice_in_dim(
+            whole, from_left, (place - step) % peers * extent, axis=0
+        )
+        if step < peers - half:
+            from_right = lax.ppermute(from_right, "seq", behind)
+            whole = lax.dynamic_update_slice_in_dim(
+                whole, from_right, (place + step) % peers * extent, axis=0
+            )
+    every_row = whole
     column_block = jnp.dot(every_row, out_weight, preferred_element_type=jnp.float32)
     partial_terms = lax.all_to_all(column_block, "seq", split_axis=0, concat_axis=1, tiled=True)
     summed = lax.psum_scatter(partial_terms, "tp", scatter_dimension=1, tiled=True)

time: 532 us -> 635 us (1.19)
  local copies, waits for them, and re-layouts: 41.2 us -> 104 us
  waiting for transfers between devices: 153 us -> 189 us
  starting transfers between devices: 0.26 us -> 12.2 us
  blocking collectives: 269 us -> 262 us
    ppermute x0 -> x15, waiting for transfers between devices: none -> 179 us  [the longest x8 178 us: local(): from_left = lax.ppermute(from_left, 'seq', ahead)]
    all_gather x1 -> x0, waiting for transfers between devices: 143 us -> none  [local(): every_row = lax.all_gather(attention_all, 'seq', axis=0, tiled=True)]
    dynamic_update_slice x0 -> x16, local copies, waits for them, and re-layouts: none -> 66.6 us  [the longest x8 33.2 us: local(): lax.dynamic_update_slice_in_dim(whole, from_left, (place - step) % peers...]
    all_to_all x1, blocking collectives: 80.1 us -> 65 us  [local(): lax.all_to_all(column_block, 'seq', split_axis=0, concat_axis=1, tiled=True)]
    ppermute x0 -> x15, starting transfers between devices: none -> 12.1 us  [the longest x7 12.1 us: local(): from_right = lax.ppermute(from_right, 'seq', behind)]
    unnamed x37 -> x54, local copies, waits for them, and re-layouts: 16.2 us -> 7.48 us
    psum x1, blocking collectives: 74.1 us -> 82.2 us  [local(): lax.psum((decode_sum * factors, decode_mixed * factors[..., None]), 'seq')]
  transfers between devices with their start and end apart: 2 -> 16, of which waited for: 2 -> 10; matrix products, arithmetic and copies ran while one was open for 0% -> 11% of each run, Pallas kernels for 0% -> 0%
where the time goes in v1:
time: 635 us; the launch traced here: 633 us
  blocking collectives  262 us (41%)
  waiting for transfers between devices  189 us (30%)
  local copies, waits for them, and re-layouts  104 us (16%)
  matrix products  43.1 us (7%)
  between operations  14.4 us (2%)
  starting transfers between devices  12.2 us (2%)
  other arithmetic  8.21 us (1%)
    ppermute x8, waiting for transfers between devices, local(): from_left = lax.ppermute(from_left, 'seq', ahead)  178 us
    psum x1, blocking collectives, local(): lax.psum((decode_sum * factors, decode_mixed * factors[..., None]), 'seq')  82.2 us
    all_to_all x1, blocking collectives, local(): lax.all_to_all(column_block, 'seq', split_axis=0, concat_axis=1, tiled=True)  65 us
    unnamed x1, blocking collectives  49.9 us
    dynamic_update_slice x8, local copies, waits for them, and re-layouts, local(): lax.dynamic_update_slice_in_dim(whole, from_left, (place - step) % peers...  33.2 us
    pmax x1, blocking collectives, local(): best = lax.pmax(decode_max, 'seq')  31.6 us
    all_gather x1, blocking collectives, local(): lax.all_gather(prefill_out[span_len - 1:], ('seq', 'tp'), axis=0, tiled=T...  31.5 us
    dynamic_update_slice x7, local copies, waits for them, and re-layouts, local(): lax.dynamic_update_slice_in_dim(whole, from_right, (place + step) % peers...  29.4 us
  transfers between devices with their start and end apart: 16, of which 10 were waited for; matrix products, arithmetic and copies ran while one was open for 11% of the time, Pallas kernels for 0%

profile of v1, /device:TPU:10, one launch (start us, length us, event | category | flops | bytes accessed | tf_op | source)
XLA Modules:
  0.0 633.1 jit_solution(16869608849481242092)
XLA Ops:
  20.1 7.5 %fusion.59 = (f32[4,5,128]{2,1,0:T(8,128)S(1)}, bf16[4,5,128,896]{2,3,1,0:T(8,128)(2,1)}) fusion(pred[128,896]{0,1:T(8,128)(4,1)S(1)} %fusion.31, bf16[128,4,5,128]{0,3,2,1:T(8,128)(2,1)} %bitcast.90, bf16[128,4,128]{2,0,1:T(8,128)(2,1)S(1)} %copy.57, bf16[768,4,128]{2,0,1:T(8,128)(2,1)} %copy.56), kind=kOutput, calls=%fused_computation.82 | convolution fusion | flops 602801024 | bytes 6285312 | tf_op jit(solution)/shard_map/sub | solution.py:85
  37.9 31.6 %pmax.7 = f32[4,4,5]{2,1,0:T(4,128)S(1)} all-reduce(f32[4,4,5]{2,1,0:T(4,128)S(1)} %get-tuple-element.62), channel_id=1, replica_groups=mesh['seq'=16,'tp'=2] {'seq'}, use_global_device_ids=true, to_apply=%region_3.4 | all-reduce | flops 80 | bytes 640 | tf_op jit(solution)/shard_map/pmax | solution.py:119
  71.2 82.2 %all-reduce.3 = (f32[4,4,5,128]{3,2,1,0:T(8,128)S(1)}, f32[4,4,5]{2,1,0:T(4,128)S(1)}) all-reduce(f32[4,4,5,128]{3,2,1,0:T(8,128)S(1)} %convolution_multiply_fusion.1, f32[4,4,5]{2,1,0:T(4,128)S(1)} %bitcast.98), channel_id=1, replica_groups=mesh['seq'=16,'tp'=2] {'seq'}, use_global_device_ids=true, to_apply=%region_4.5 | all-reduce | flops 10320 | bytes 82560 | tf_op jit(solution)/shard_map/psum | solution.py:121
  155.7 27.6 %collective-permute-done = bf16[132,2560]{1,0:T(8,128)(2,1)S(1)} collective-permute-done((bf16[132,2560]{1,0:T(8,128)(2,1)S(1)}, bf16[132,2560]{1,0:T(8,128)(2,1)S(1)}, u32[]{:S(2)}, u32[]{:S(2)}) %collective-permute-start) | collective-permute-done | bytes 675872 | tf_op jit(solution)/shard_map/ppermute | solution.py:148
  185.3 28.7 %collective-permute-done.2 = bf16[132,2560]{1,0:T(8,128)(2,1)S(1)} collective-permute-done((bf16[132,2560]{1,0:T(8,128)(2,1)S(1)}, bf16[132,2560]{1,0:T(8,128)(2,1)S(1)}, u32[]{:S(2)}, u32[]{:S(2)}) %collective-permute-start.2) | collective-permute-done | bytes 675872 | tf_op jit(solution)/shard_map/ppermute | solution.py:148
  216.1 28.6 %collective-permute-done.4 = bf16[132,2560]{1,0:T(8,128)(2,1)S(1)} collective-permute-done((bf16[132,2560]{1,0:T(8,128)(2,1)S(1)}, bf16[132,2560]{1,0:T(8,128)(2,1)S(1)}, u32[]{:S(2)}, u32[]{:S(2)}) %collective-permute-start.4) | collective-permute-done | bytes 675872 | tf_op jit(solution)/shard_map/ppermute | solution.py:148
  246.8 29.0 %collective-permute-done.6 = bf16[132,2560]{1,0:T(8,128)(2,1)S(1)} collective-permute-done((bf16[132,2560]{1,0:T(8,128)(2,1)S(1)}, bf16[132,2560]{1,0:T(8,128)(2,1)S(1)}, u32[]{:S(2)}, u32[]{:S(2)}) %collective-permute-start.6) | collective-permute-done | bytes 675872 | tf_op jit(solution)/shard_map/ppermute | solution.py:148
  277.9 28.6 %collective-permute-done.8 = bf16[132,2560]{1,0:T(8,128)(2,1)S(1)} collective-permute-done((bf16[132,2560]{1,0:T(8,128)(2,1)S(1)}, bf16[132,2560]{1,0:T(8,128)(2,1)S(1)}, u32[]{:S(2)}, u32[]{:S(2)}) %collective-permute-start.8) | collective-permute-done | bytes 675872 | tf_op jit(solution)/shard_map/ppermute | solution.py:148
  309.3 20.0 %collective-permute-done.10 = bf16[132,2560]{1,0:T(8,128)(2,1)S(1)} collective-permute-done((bf16[132,2560]{1,0:T(8,128)(2,1)S(1)}, bf16[132,2560]{1,0:T(8,128)(2,1)S(1)}, u32[]{:S(2)}, u32[]{:S(2)}) %collective-permute-start.10) | collective-permute-done | bytes 675872 | tf_op jit(solution)/shard_map/ppermute | solution.py:148
  332.6 15.2 %collective-permute-done.12 = bf16[132,2560]{1,0:T(8,128)(2,1)} collective-permute-done((bf16[132,2560]{1,0:T(8,128)(2,1)S(1)}, bf16[132,2560]{1,0:T(8,128)(2,1)}, u32[]{:S(2)}, u32[]{:S(2)}) %collective-permute-start.12) | collective-permute-done | bytes 675872 | tf_op jit(solution)/shard_map/ppermute | solution.py:148
  347.8 4.8 broadcast_in_dim.87
  360.6 4.3 dynamic_update_slice.50
  365.0 4.3 dynamic_update_slice.51
  377.2 4.3 dynamic_update_slice.54
  402.2 4.3 dynamic_update_slice.60
  410.7 4.3 dynamic_update_slice.62
  415.0 4.3 dynamic_update_slice.63
  419.3 10.3 %fusion.62 = f32[2112,320]{1,0:T(8,128)} fusion(bf16[2112,2560]{1,0:T(8,128)(2,1)} %dynamic_update_slice.63, bf16[2560,320]{0,1:T(8,128)(2,1)S(1)} %copy-done), kind=kOutput, calls=%fused_computation.85 | convolution fusion | flops 3460300800 | bytes 15155200 | tf_op jit(solution)/shard_map/dot_general | solution.py:158
  433.8 65.0 %all_to_all.19 = f32[16,132,320]{2,1,0:T(8,128)S(1)} all-to-all(f32[16,132,320]{2,1,0:T(8,128)} %all_to_all.14), channel_id=1, replica_groups=mesh['seq'=16,'tp'=2] {'seq'}, dimensions={0} | all-to-all | bytes 5406720 | tf_op jit(solution)/shard_map/all_to_all | solution.py:159
  501.1 4.8 all_to_all.17
  505.9 10.2 %reduce-scatter.2.cloned.1.call-done = f32[132,2560]{1,0:T(8,128)} async-done(((f32[132,5120]{1,0:T(8,128)}), f32[132,2560]{1,0:T(8,128)}) %reduce-scatter.2.cloned.1.call-update) | async-done | bytes 1351696 | tf_op jit(solution)/shard_map/reduce_scatter | solution.py:160
  517.6 31.5 %all-gather.2 = bf16[32,1,2560]{2,1,0:T(2,128)(2,1)S(1)} all-gather(bf16[1,1,2560]{2,1,0:T(2,128)(2,1)S(1)} %slice_bitcast_fusion), channel_id=1, replica_groups=mesh['seq'=16,'tp'=2] {'seq','tp'}, dimensions={0}, use_global_device_ids=true | all-gather | bytes 168960 | tf_op jit(solution)/shard_map/all_gather | solution.py:165
  552.4 19.8 %fusion.60 = (f32[20]{0:T(128)S(1)}, f32[20,4752]{1,0:T(8,128)S(1)}) fusion(bf16[5120,4752]{0,1:T(8,128)(2,1)} %param.29, f32[5120]{0:T(1024)S(1)} %convert_element_type.43, f32[20]{0:T(128)S(1)} %add_rsqrt_fusion, bf16[16,5120]{1,0:T(8,128)(2,1)S(1)} %reshape.110, bf16[4,5120]{1,0:T(4,128)(2,1)S(1)} %all_gather.18), kind=kOutput, calls=%fused_computation.83 | convolution fusion | flops 974021440 | bytes 49266080 | tf_op jit(solution)/shard_map/dot_general | solution.py:176
  573.0 49.9 %all-reduce.2 = (f32[640]{0:T(1024)S(1)}, f32[640]{0:T(1024)S(1)}) all-reduce(f32[640]{0:T(1024)S(1)} %dynamic-update-slice, f32[640]{0:T(1024)S(1)} %dynamic-update-slice.1), channel_id=2, replica_groups=mesh['seq'=16,'tp'=2] {'seq','tp'}, use_global_device_ids=true, to_apply=%add | all-reduce | flops 1280 | bytes 10240
  (176 shorter events, 98.6 us)
Async XLA Ops:
  7.2 412.1 %copy-start = (bf16[2560,320]{0,1:T(8,128)(2,1)S(1)}, bf16[2560,320]{0,1:T(8,128)(2,1)}, u32[]{:S(2)}) copy-start(bf16[2560,320]{0,1:T(8,128)(2,1)} %param.27) | copy-start | bytes 4915204
  7.2 508.9 %reduce-scatter.2.cloned.1.call-start = ((), (), s32[]{:S(2)}) async-start(), calls=%async_computation.2 | async-start | bytes 4177920 | tf_op jit(solution)/shard_map/reduce_scatter | solution.py:160
  33.1 36.8 %copy-start.21 = (bf16[2,4,512]{2,1,0:T(4,128)(2,1)S(1)}, bf16[2,4,512]{2,1,0:T(4,128)(2,1)}, u32[]{:S(2)}) copy-start(bf16[2,4,512]{2,1,0:T(4,128)(2,1)} %param.23) | copy-start | bytes 24580
  153.6 29.7 %collective-permute-start = (bf16[132,2560]{1,0:T(8,128)(2,1)S(1)}, bf16[132,2560]{1,0:T(8,128)(2,1)S(1)}, u32[]{:S(2)}, u32[]{:S(2)}) collective-permute-start(bf16[132,2560]{1,0:T(8,128)(2,1)S(1)} %pad_maximum_fusion), channel_id=1, source_target_pairs={{0,2},{2,4},{4,6},{6,8},{8,10},{10,12},{12,14},{14,16},{16,18},{18... | collective-permute-start | bytes 2027528 | tf_op jit(solution)/shard_map/ppermute | solution.py:148
  153.7 29.6 %collective-permute-start.1 = (bf16[132,2560]{1,0:T(8,128)(2,1)S(1)}, bf16[132,2560]{1,0:T(8,128)(2,1)S(1)}, u32[]{:S(2)}, u32[]{:S(2)}) collective-permute-start(bf16[132,2560]{1,0:T(8,128)(2,1)S(1)} %pad_maximum_fusion), channel_id=1, source_target_pairs={{0,30},{2,0},{4,2},{6,4},{8,6},{10,8},{12,10},{14,12},{16,14},{18,... | collective-permute-start | bytes 2027528 | tf_op jit(solution)/shard_map/ppermute | solution.py:153
  183.3 30.7 %collective-permute-start.2 = (bf16[132,2560]{1,0:T(8,128)(2,1)S(1)}, bf16[132,2560]{1,0:T(8,128)(2,1)S(1)}, u32[]{:S(2)}, u32[]{:S(2)}) collective-permute-start(bf16[132,2560]{1,0:T(8,128)(2,1)S(1)} %collective-permute-done), channel_id=1, source_target_pairs={{0,2},{2,4},{4,6},{6,8},{8,10},{10,12},{12,14},{14,16},{16,18},{18... | collective-permute-start | bytes 2027528 | tf_op jit(solution)/shard_map/ppermute | solution.py:148
  183.3 30.7 %copy-start.2 = (bf16[132,2560]{1,0:T(8,128)(2,1)}, bf16[132,2560]{1,0:T(8,128)(2,1)S(1)}, u32[]{:S(2)}) copy-start(bf16[132,2560]{1,0:T(8,128)(2,1)S(1)} %collective-permute-done.1) | copy-start | bytes 2027524
  183.3 30.7 %collective-permute-start.3 = (bf16[132,2560]{1,0:T(8,128)(2,1)S(1)}, bf16[132,2560]{1,0:T(8,128)(2,1)S(1)}, u32[]{:S(2)}, u32[]{:S(2)}) collective-permute-start(bf16[132,2560]{1,0:T(8,128)(2,1)S(1)} %collective-permute-done.1), channel_id=1, source_target_pairs={{0,30},{2,0},{4,2},{6,4},{8,6},{10,8},{12,10},{14,12},{16,14},{18,... | collective-permute-start | bytes 2027528 | tf_op jit(solution)/shard_map/ppermute | solution.py:153
  214.0 30.7 %collective-permute-start.4 = (bf16[132,2560]{1,0:T(8,128)(2,1)S(1)}, bf16[132,2560]{1,0:T(8,128)(2,1)S(1)}, u32[]{:S(2)}, u32[]{:S(2)}) collective-permute-start(bf16[132,2560]{1,0:T(8,128)(2,1)S(1)} %collective-permute-done.2), channel_id=1, source_target_pairs={{0,2},{2,4},{4,6},{6,8},{8,10},{10,12},{12,14},{14,16},{16,18},{18... | collective-permute-start | bytes 2027528 | tf_op jit(solution)/shard_map/ppermute | solution.py:148
  214.9 29.9 %copy-start.4 = (bf16[132,2560]{1,0:T(8,128)(2,1)}, bf16[132,2560]{1,0:T(8,128)(2,1)S(1)}, u32[]{:S(2)}) copy-start(bf16[132,2560]{1,0:T(8,128)(2,1)S(1)} %collective-permute-done.3) | copy-start | bytes 2027524
  214.9 29.9 %collective-permute-start.5 = (bf16[132,2560]{1,0:T(8,128)(2,1)S(1)}, bf16[132,2560]{1,0:T(8,128)(2,1)S(1)}, u32[]{:S(2)}, u32[]{:S(2)}) collective-permute-start(bf16[132,2560]{1,0:T(8,128)(2,1)S(1)} %collective-permute-done.3), channel_id=1, source_target_pairs={{0,30},{2,0},{4,2},{6,4},{8,6},{10,8},{12,10},{14,12},{16,14},{18,... | collective-permute-start | bytes 2027528 | tf_op jit(solution)/shard_map/ppermute | solution.py:153
  244.7 31.1 %collective-permute-start.6 = (bf16[132,2560]{1,0:T(8,128)(2,1)S(1)}, bf16[132,2560]{1,0:T(8,128)(2,1)S(1)}, u32[]{:S(2)}, u32[]{:S(2)}) collective-permute-start(bf16[132,2560]{1,0:T(8,128)(2,1)S(1)} %collective-permute-done.4), channel_id=1, source_target_pairs={{0,2},{2,4},{4,6},{6,8},{8,10},{10,12},{12,14},{14,16},{16,18},{18... | collective-permute-start | bytes 2027528 | tf_op jit(solution)/shard_map/ppermute | solution.py:148
  245.6 30.2 %copy-start.8 = (bf16[132,2560]{1,0:T(8,128)(2,1)}, bf16[132,2560]{1,0:T(8,128)(2,1)S(1)}, u32[]{:S(2)}) copy-start(bf16[132,2560]{1,0:T(8,128)(2,1)S(1)} %collective-permute-done.5) | copy-start | bytes 2027524
  245.6 30.2 %collective-permute-start.7 = (bf16[132,2560]{1,0:T(8,128)(2,1)S(1)}, bf16[132,2560]{1,0:T(8,128)(2,1)S(1)}, u32[]{:S(2)}, u32[]{:S(2)}) collective-permute-start(bf16[132,2560]{1,0:T(8,128)(2,1)S(1)} %collective-permute-done.5), channel_id=1, source_target_pairs={{0,30},{2,0},{4,2},{6,4},{8,6},{10,8},{12,10},{14,12},{16,14},{18,... | collective-permute-start | bytes 2027528 | tf_op jit(solution)/shard_map/ppermute | solution.py:153
  275.8 30.7 %collective-permute-start.8 = (bf16[132,2560]{1,0:T(8,128)(2,1)S(1)}, bf16[132,2560]{1,0:T(8,128)(2,1)S(1)}, u32[]{:S(2)}, u32[]{:S(2)}) collective-permute-start(bf16[132,2560]{1,0:T(8,128)(2,1)S(1)} %collective-permute-done.6), channel_id=1, source_target_pairs={{0,2},{2,4},{4,6},{6,8},{8,10},{10,12},{12,14},{14,16},{16,18},{18... | collective-permute-start | bytes 2027528 | tf_op jit(solution)/shard_map/ppermute | solution.py:148
  276.7 29.8 %copy-start.10 = (bf16[132,2560]{1,0:T(8,128)(2,1)}, bf16[132,2560]{1,0:T(8,128)(2,1)S(1)}, u32[]{:S(2)}) copy-start(bf16[132,2560]{1,0:T(8,128)(2,1)S(1)} %collective-permute-done.7) | copy-start | bytes 2027524
  276.7 30.1 %collective-permute-start.9 = (bf16[132,2560]{1,0:T(8,128)(2,1)S(1)}, bf16[132,2560]{1,0:T(8,128)(2,1)S(1)}, u32[]{:S(2)}, u32[]{:S(2)}) collective-permute-start(bf16[132,2560]{1,0:T(8,128)(2,1)S(1)} %collective-permute-done.7), channel_id=1, source_target_pairs={{0,30},{2,0},{4,2},{6,4},{8,6},{10,8},{12,10},{14,12},{16,14},{18,... | collective-permute-start | bytes 2027528 | tf_op jit(solution)/shard_map/ppermute | solution.py:153
  306.5 22.7 %collective-permute-start.10 = (bf16[132,2560]{1,0:T(8,128)(2,1)S(1)}, bf16[132,2560]{1,0:T(8,128)(2,1)S(1)}, u32[]{:S(2)}, u32[]{:S(2)}) collective-permute-start(bf16[132,2560]{1,0:T(8,128)(2,1)S(1)} %collective-permute-done.8), channel_id=1, source_target_pairs={{0,2},{2,4},{4,6},{6,8},{8,10},{10,12},{12,14},{14,16},{16,18},{18... | collective-permute-start | bytes 2027528 | tf_op jit(solution)/shard_map/ppermute | solution.py:148
  307.4 22.6 %collective-permute-start.11 = (bf16[132,2560]{1,0:T(8,128)(2,1)S(1)}, bf16[132,2560]{1,0:T(8,128)(2,1)}, u32[]{:S(2)}, u32[]{:S(2)}) collective-permute-start(bf16[132,2560]{1,0:T(8,128)(2,1)S(1)} %collective-permute-done.9), channel_id=1, source_target_pairs={{0,30},{2,0},{4,2},{6,4},{8,6},{10,8},{12,10},{14,12},{16,14},{18,... | collective-permute-start | bytes 2027528 | tf_op jit(solution)/shard_map/ppermute | solution.py:153
  329.2 18.6 %collective-permute-start.12 = (bf16[132,2560]{1,0:T(8,128)(2,1)S(1)}, bf16[132,2560]{1,0:T(8,128)(2,1)}, u32[]{:S(2)}, u32[]{:S(2)}) collective-permute-start(bf16[132,2560]{1,0:T(8,128)(2,1)S(1)} %collective-permute-done.10), channel_id=1, source_target_pairs={{0,2},{2,4},{4,6},{6,8},{8,10},{10,12},{12,14},{14,16},{16,18},{18... | collective-permute-start | bytes 2027528 | tf_op jit(solution)/shard_map/ppermute | solution.py:148
  330.1 80.6 %collective-permute-start.13 = (bf16[132,2560]{1,0:T(8,128)(2,1)}, bf16[132,2560]{1,0:T(8,128)(2,1)}, u32[]{:S(2)}, u32[]{:S(2)}) collective-permute-start(bf16[132,2560]{1,0:T(8,128)(2,1)} %collective-permute-done.11), channel_id=1, source_target_pairs={{0,30},{2,0},{4,2},{6,4},{8,6},{10,8},{12,10},{14,12},{16,14},{18,... | collective-permute-start | bytes 2027528 | tf_op jit(solution)/shard_map/ppermute | solution.py:153
  347.8 67.2 %collective-permute-start.14 = (bf16[132,2560]{1,0:T(8,128)(2,1)}, bf16[132,2560]{1,0:T(8,128)(2,1)}, u32[]{:S(2)}, u32[]{:S(2)}) collective-permute-start(bf16[132,2560]{1,0:T(8,128)(2,1)} %collective-permute-done.12), channel_id=1, source_target_pairs={{0,2},{2,4},{4,6},{6,8},{8,10},{10,12},{12,14},{14,16},{16,18},{18... | collective-permute-start | bytes 2027528 | tf_op jit(solution)/shard_map/ppermute | solution.py:148
  517.6 54.6 %copy-start.17 = (bf16[4,2560]{1,0:T(4,128)(2,1)}, bf16[4,2560]{1,0:T(4,128)(2,1)S(1)}, u32[]{:S(2)}) copy-start(bf16[4,2560]{1,0:T(4,128)(2,1)S(1)} %slice.70) | copy-start | bytes 61444
  552.4 73.9 %copy-start.1 = (bf16[2560,320]{0,1:T(8,128)(2,1)S(1)}, bf16[2560,320]{0,1:T(8,128)(2,1)}, u32[]{:S(2)}) copy-start(bf16[2560,320]{0,1:T(8,128)(2,1)} %param.27) | copy-start | bytes 4915204
  (15 other events, 122.9 us)
Sparse Core Ops, SparseCore 0:
  506.0 10.0 reduce-scatter.1
